TPU v7x, 256 devices: a whole 4x4x8 slice. The times are simulated.
256 devices in a mesh: replica: 8 (over y, core), fsdp: 32 (over x, z).
Axes of the slice: x: 4, y: 4, z: 8, core: 2. Of those that a mesh axis runs over, the one named last changes fastest.
Arguments:
- anchor_params: bfloat16 [24, 512, 4096], P(None, 'fsdp')
- replica_params: bfloat16 [8, 24, 512, 4096], P('replica', None, 'fsdp')
- projection: bfloat16 [4096, 384], replicated
- momentum: float32 [24, 512, 384], P(None, 'fsdp'), may hold values from -1.8 to 1.8
- rate_table: float32 [4, 6], replicated, may hold values from 0.1 to 1
- owner_list: int32 [24], replicated, may hold values from 0 to 31, as said below
- layer_kind: int32 [24, 2], replicated, may hold values from 0 to 5, as said below
Outputs:
- new_params: bfloat16 [24, 512, 4096], P(None, 'fsdp')
- new_momentum: float32 [24, 512, 384], P(None, 'fsdp')
Inputs may be any that keep to these rules, and one draw needn't show every extreme that they name: `owner_list`: no fsdp index is named more than 2 times, and in every draw some index is named exactly 2 times. `layer_kind`: column 0 is a layer, column 1 a kind below 6; each layer has 6 rows, and no two rows are equal.
All inputs are finite; a program needn't handle non-finite values.
Results may differ from a plain program's by a relative error of at most 0.0055.
Values may be sent and summed in bfloat16 or wider, within the bound.
No kernel may reach another device: no remote copies, remote signals or barrier semaphores. Data moves between devices by JAX's collectives and lax.ppermute only.
A program may use at most 128 MiB of HBM per device.

v0:
```python
import jax
import jax.numpy as jnp
from jax import lax
from jax.sharding import PartitionSpec as P

OUTER_MOMENTUM = 0.9
EPSILON = 1e-06


def decompress(direction, projection):
    flattened = direction.reshape(-1, direction.shape[-1])
    return lax.dot_general(
        flattened, projection, (((1,), (1,)), ((), ())), preferred_element_type=jnp.float32
    ).astype(jnp.bfloat16)


def local(anchor_params, replica_params, projection, momentum, rate_table, owner_list, layer_kind):
    matrices, rows_dev, model_width = anchor_params.shape
    rank_dim = projection.shape[1]
    fsdp_size = lax.axis_size("fsdp")
    own_bound = max(2, (matrices + fsdp_size - 1) // fsdp_size + 1)
    all_rows = rows_dev * fsdp_size
    highest = lax.Precision.HIGHEST
    pseudo_grad = (
        anchor_params.astype(jnp.float32) - replica_params[0].astype(jnp.float32)
    ).astype(jnp.bfloat16)
    compressed = jnp.dot(
        pseudo_grad.reshape(matrices * rows_dev, model_width),
        projection,
        preferred_element_type=jnp.float32,
    )
    summed = lax.psum(compressed.reshape(matrices, rows_dev, rank_dim), "replica")
    outer_grad = summed / lax.axis_size("replica")
    new_momentum = OUTER_MOMENTUM * momentum + outer_grad
    outer_step = outer_grad + OUTER_MOMENTUM * new_momentum
    same_group = (owner_list[:, None] == owner_list[None, :]).astype(jnp.float32)
    layer_onehot = (layer_kind[:, 0:1] == jnp.arange(rate_table.shape[0])[None, :]).astype(
        jnp.float32
    )
    kind_onehot = (layer_kind[:, 1:2] == jnp.arange(rate_table.shape[1])[None, :]).astype(
        jnp.float32
    )
    outer_rate = jnp.sum(jnp.dot(layer_onehot, rate_table, precision=highest) * kind_onehot, axis=1)
    own_index = lax.axis_index("fsdp")
    earlier = jnp.arange(matrices)[:, None] > jnp.arange(matrices)[None, :]
    position = jnp.sum(jnp.where(earlier, same_group, 0.0), axis=1).astype(jnp.int32)
    slot_of = owner_list * own_bound + position
    slot_ids = jnp.arange(fsdp_size * own_bound, dtype=jnp.int32)
    picker = (slot_ids[:, None] == slot_of[None, :]).astype(jnp.float32)
    outgoing = jnp.dot(picker, outer_step.reshape(matrices, -1), precision=highest).reshape(
        fsdp_size, own_bound, rows_dev, rank_dim
    )
    incoming = lax.all_to_all(outgoing, "fsdp", split_axis=0, concat_axis=0, tiled=True)
    own_slots = own_index * own_bound + jnp.arange(own_bound, dtype=jnp.int32)
    owned_slots = (slot_of[None, :] == own_slots[:, None]).astype(jnp.float32)
    owned_count = jnp.maximum(jnp.sum(owned_slots), 1.0)
    group_squares = jnp.sum(incoming * incoming)
    scaling = lax.rsqrt(group_squares / (owned_count * (all_rows * rank_dim)) + EPSILON)
    slot_rate = jnp.dot(owned_slots, outer_rate, precision=highest)
    slot_direction = (incoming * (slot_rate * scaling)[None, :, None, None]).astype(jnp.bfloat16)
    back_picker = picker.T.astype(jnp.bfloat16)
    slot_update = decompress(slot_direction, projection).reshape(
        fsdp_size, own_bound, rows_dev, model_width
    )
    returned = lax.all_to_all(slot_update, "fsdp", split_axis=0, concat_axis=0, tiled=True)
    update = (
        jnp.dot(
            back_picker,
            returned.reshape(fsdp_size * own_bound, -1),
            preferred_element_type=jnp.float32,
        )
        .astype(jnp.bfloat16)
        .reshape(matrices, rows_dev, model_width)
    )
    new_params = (anchor_params.astype(jnp.float32) - update.astype(jnp.float32)).astype(
        jnp.bfloat16
    )
    return (new_params, new_momentum)


def solution(mesh):
    placed = (
        P(None, "fsdp", None),
        P("replica", None, "fsdp", None),
        P(),
        P(None, "fsdp", None),
        P(),
        P(),
        P(),
    )
    return jax.shard_map(
        local,
        mesh=mesh,
        in_specs=placed,
        out_specs=(P(None, "fsdp", None), P(None, "fsdp", None)),
        check_vma=False,
    )
```

profile of v0, /device:TPU:24, one launch (start us, length us, event | category | flops | bytes accessed | tf_op | source)
XLA Modules:
  0.0 368.5 jit_solution(15477138471797277751)
XLA Ops:
  7.2 0.0 copy-start
  7.2 0.0 all-reduce.2.cloned.1.call-start
  7.2 1.8 copy-done
  9.1 5.4 %fusion.3 = f32[24,16,384]{2,1,0:T(8,128)} fusion(bf16[24,16,4096]{2,1,0:T(8,128)(2,1)} %param.7, bf16[1,24,16,4096]{3,2,1,0:T(8,128)(2,1)} %param.8, bf16[4096,384]{1,0:T(8,128)(2,1)S(1)} %copy-done), kind=kOutput, calls=%fused_computation.7 | convolution fusion | flops 1214251008 | bytes 10027008 | tf_op jit(solution)/shard_map/dot_general | solution.py:27
  14.5 0.0 all-reduce.2.cloned.1.call-update
  14.5 0.2 select_reduce_fusion
  14.7 66.8 %all-reduce.2.cloned.1.call-done = f32[24,16,384]{2,1,0:T(8,128)} async-done(((f32[24,16,384]{2,1,0:T(8,128)}), f32[24,16,384]{2,1,0:T(8,128)}) %all-reduce.2.cloned.1.call-update) | async-done | bytes 589840 | tf_op jit(solution)/shard_map/psum | solution.py:32
  81.6 2.2 multiply_add_fusion
  83.7 0.9 fusion.9
  84.6 0.0 copy-start.2
  84.7 2.1 copy.14
  86.7 9.9 %all-to-all-start = ((f32[32,2,16,384]{3,2,1,0:T(8,128)}), f32[32,2,16,384]{3,2,1,0:T(8,128)}, u32[]{:S(2)}, u32[]{:S(2)}) async-start(f32[32,2,16,384]{3,2,1,0:T(8,128)} %copy.14), calls=%async_computation | async-start | bytes 3145728 | tf_op jit(solution)/shard_map/all_to_all | solution.py:53
  96.7 0.7 fusion.18
  98.0 0.2 fusion.7
  98.2 38.5 %all-to-all-done = f32[32,2,16,384]{3,2,1,0:T(8,128)} async-done(((f32[32,2,16,384]{3,2,1,0:T(8,128)}), f32[32,2,16,384]{3,2,1,0:T(8,128)}, u32[]{:S(2)}, u32[]{:S(2)}) %all-to-all-start) | async-done | bytes 1572896 | tf_op jit(solution)/shard_map/all_to_all | solution.py:53
  136.7 2.4 multiply_reduce_fusion
  139.8 0.2 fusion.8
  140.0 1.6 multiply_convert_fusion
  141.6 4.8 %convolution_convert_fusion.1 = bf16[1024,4096]{1,0:T(8,128)(2,1)S(1)} fusion(bf16[1024,384]{1,0:T(8,128)(2,1)S(1)} %bitcast.56, bf16[4096,384]{1,0:T(8,128)(2,1)S(1)} %copy-done), kind=kOutput, calls=%fused_computation.4 | convolution fusion | flops 3225419776 | bytes 12320768 | tf_op jit(solution)/shard_map/dot_general | solution.py:12
  146.4 192.3 %all_to_all.10 = bf16[32,2,16,4096]{3,2,1,0:T(8,128)(2,1)} all-to-all(bf16[32,2,16,4096]{3,2,1,0:T(8,128)(2,1)S(1)} %bitcast.54), channel_id=1, replica_groups=mesh['replica'=8,'fsdp'=32] {'fsdp'}, dimensions={0} | all-to-all | bytes 16777216 | tf_op jit(solution)/shard_map/all_to_all | solution.py:65
  338.8 12.0 %copy.18 = bf16[8,8,16,4096]{3,1,2,0:T(8,128)(2,1)} copy(bf16[8,8,16,4096]{3,2,1,0:T(8,128)(2,1)} %bitcast.52) | data formatting | bytes 16777216
  350.7 4.7 %fusion = f32[24,65536]{1,0:T(8,128)S(1)} fusion(bf16[64,65536]{1,0:T(8,128)(2,1)} %bitcast.51, s32[24]{0:T(128)S(1)} %convert_add_fusion), kind=kOutput, calls=%fused_computation.1 | convolution fusion | flops 204476928 | bytes 14680160 | tf_op jit(solution)/shard_map/dot_general | solution.py:67
  355.4 3.6 copy.19
  359.0 2.6 fusion.2
  (11 shorter events, 0.0 us)
Async XLA Ops:
  7.2 1.9 copy-start
  7.2 7.4 %copy-start.4 = (s32[24]{0:T(128)S(1)}, s32[24]{0:T(128)}, u32[]{:S(2)}) copy-start(s32[24]{0:T(128)} %param.12) | copy-start | bytes 292
  7.2 74.4 %all-reduce.2.cloned.1.call-start = ((), (), s32[]{:S(2)}) async-start(), calls=%async_computation.2 | async-start | bytes 1179648 | tf_op jit(solution)/shard_map/psum | solution.py:32
  84.6 13.3 %copy-start.2 = (s32[24,2]{0,1:T(2,128)S(1)}, s32[24,2]{0,1:T(2,128)}, u32[]{:S(2)}) copy-start(s32[24,2]{0,1:T(2,128)} %param.13) | copy-start | bytes 580
  84.7 13.4 %copy-start.3 = (f32[4,6]{1,0:T(4,128)S(1)}, f32[4,6]{1,0:T(4,128)}, u32[]{:S(2)}) copy-start(f32[4,6]{1,0:T(4,128)} %param.11) | copy-start | bytes 292
  86.7 50.0 %all-to-all-start = ((f32[32,2,16,384]{3,2,1,0:T(8,128)}), f32[32,2,16,384]{3,2,1,0:T(8,128)}, u32[]{:S(2)}, u32[]{:S(2)}) async-start(f32[32,2,16,384]{3,2,1,0:T(8,128)} %copy.14), calls=%async_computation | async-start | bytes 3145728 | tf_op jit(solution)/shard_map/all_to_all | solution.py:53
  355.4 3.7 copy-start.1
Sparse Core Ops, SparseCore 0:
  14.7 66.8 all-reduce.1
where the time goes:
time: 369 us
  blocking collectives  192 us (52%)
  waiting for transfers between devices  105 us (28%)
  local copies, waits for them, and re-layouts  19.5 us (5%)
  matrix products  16.2 us (4%)
  between operations  15.5 us (4%)
  starting transfers between devices  9.97 us (3%)
  other arithmetic  9.73 us (3%)
    all_to_all x1, blocking collectives, local(): lax.all_to_all(slot_update, 'fsdp', split_axis=0, concat_axis=0, tiled=True)  192 us
    psum x1, waiting for transfers between devices, local(): lax.psum(compressed.reshape(matrices, rows_dev, rank_dim), 'replica')  66.8 us
    all_to_all x1, waiting for transfers between devices, local(): lax.all_to_all(outgoing, 'fsdp', split_axis=0, concat_axis=0, tiled=True)  38.5 us
    unnamed x12, local copies, waits for them, and re-layouts  17.5 us
    all_to_all x1, starting transfers between devices, local(): lax.all_to_all(outgoing, 'fsdp', split_axis=0, concat_axis=0, tiled=True)  9.93 us
  transfers between devices with their start and end apart: 2, of which 2 were waited for; matrix products, arithmetic and copies ran while one was open for 0% of the time, Pallas kernels for 0%

commit v1 on v0

--- a/solution.py
+++ b/solution.py
@@ -2,6 +2,7 @@
 import jax.numpy as jnp
 from jax import lax
 from jax.sharding import PartitionSpec as P
+from jax.lax import all_gather
 
 OUTER_MOMENTUM = 0.9
 EPSILON = 1e-06
@@ -15,6 +16,11 @@
 
 
 def local(anchor_params, replica_params, projection, momentum, rate_table, owner_list, layer_kind):
+
+    def edit_the_squares(xin):
+        y = all_gather(xin, "replica").sum(axis=0)
+        return y
+
     matrices, rows_dev, model_width = anchor_params.shape
     rank_dim = projection.shape[1]
     fsdp_size = lax.axis_size("fsdp")
@@ -29,7 +35,7 @@
         projection,
         preferred_element_type=jnp.float32,
     )
-    summed = lax.psum(compressed.reshape(matrices, rows_dev, rank_dim), "replica")
+    summed = edit_the_squares(compressed.reshape(matrices, rows_dev, rank_dim))
     outer_grad = summed / lax.axis_size("replica")
     new_momentum = OUTER_MOMENTUM * momentum + outer_grad
     outer_step = outer_grad + OUTER_MOMENTUM * new_momentum

time: 369 us -> 344 us (0.932)
  waiting for transfers between devices: 105 us -> 75.6 us
    psum x1 -> x0, waiting for transfers between devices: 66.8 us -> none  [local(): lax.psum(compressed.reshape(matrices, rows_dev, rank_dim), 'replica')]
    all_gather x0 -> x1, waiting for transfers between devices: none -> 37.6 us  [edit_the_squares(): y = all_gather(xin, 'replica').sum(axis=0)]
where the time goes in v1:
time: 344 us; the launch traced here: 341 us
  blocking collectives  191 us (56%)
  waiting for transfers between devices  75.6 us (22%)
  local copies, waits for them, and re-layouts  19.5 us (6%)
  matrix products  16.2 us (5%)
  between operations  15.5 us (5%)
  other arithmetic  13.2 us (4%)
  starting transfers between devices  9.96 us (3%)
    all_to_all x1, blocking collectives, local(): lax.all_to_all(slot_update, 'fsdp', split_axis=0, concat_axis=0, tiled=True)  191 us
    all_to_all x1, waiting for transfers between devices, local(): lax.all_to_all(outgoing, 'fsdp', split_axis=0, concat_axis=0, tiled=True)  38.1 us
    all_gather x1, waiting for transfers between devices, edit_the_squares(): y = all_gather(xin, 'replica').sum(axis=0)  37.6 us
    unnamed x12, local copies, waits for them, and re-layouts  17.5 us
    all_to_all x1, starting transfers between devices, local(): lax.all_to_all(outgoing, 'fsdp', split_axis=0, concat_axis=0, tiled=True)  9.92 us
  transfers between devices with their start and end apart: 2, of which 2 were waited for; matrix products, arithmetic and copies ran while one was open for 0% of the time, Pallas kernels for 0%

profile of v1, /device:TPU:24, one launch (start us, length us, event | category | flops | bytes accessed | tf_op | source)
XLA Modules:
  0.0 341.5 jit_solution(5965996344530218006)
XLA Ops:
  7.2 0.0 copy-start
  7.2 0.0 all-gather.3.cloned.1.call-start
  7.2 1.8 copy-done
  9.1 5.4 %fusion.3 = f32[24,16,384]{2,1,0:T(8,128)} fusion(bf16[24,16,4096]{2,1,0:T(8,128)(2,1)} %param.7, bf16[1,24,16,4096]{3,2,1,0:T(8,128)(2,1)} %param.8, bf16[4096,384]{1,0:T(8,128)(2,1)S(1)} %copy-done), kind=kOutput, calls=%fused_computation.7 | convolution fusion | flops 1214251008 | bytes 10027008 | tf_op jit(solution)/shard_map/dot_general | solution.py:33
  14.5 0.0 all-gather.3.cloned.1.call-update
  14.6 0.2 select_reduce_fusion
  14.7 37.6 %all-gather.3.cloned.1.call-done = f32[192,16,384]{2,1,0:T(8,128)} async-done(((f32[24,16,384]{2,1,0:T(8,128)}), f32[192,16,384]{2,1,0:T(8,128)}) %all-gather.3.cloned.1.call-update) | async-done | bytes 4718608 | tf_op jit(solution)/shard_map/all_gather | solution.py:21
  52.3 3.5 %reduce_sum.46 = f32[24,16,384]{2,1,0:T(8,128)} reduce(f32[8,24,16,384]{3,2,1,0:T(8,128)} %bitcast.56, f32[]{:T(128)} %constant.9.clone.1), dimensions={0}, to_apply=%region_1.0 | reduce | flops 1032192 | bytes 5308420 | tf_op jit(solution)/shard_map/reduce_sum | solution.py:21
  55.8 2.2 multiply_add_fusion
  58.0 0.9 fusion.9
  58.9 2.1 copy.14
  61.0 9.9 %all-to-all-start = ((f32[32,2,16,384]{3,2,1,0:T(8,128)}), f32[32,2,16,384]{3,2,1,0:T(8,128)}, u32[]{:S(2)}, u32[]{:S(2)}) async-start(f32[32,2,16,384]{3,2,1,0:T(8,128)} %copy.14), calls=%async_computation | async-start | bytes 3145728 | tf_op jit(solution)/shard_map/all_to_all | solution.py:59
  70.9 0.7 fusion.18
  72.2 0.2 fusion.7
  72.5 38.1 %all-to-all-done = f32[32,2,16,384]{3,2,1,0:T(8,128)} async-done(((f32[32,2,16,384]{3,2,1,0:T(8,128)}), f32[32,2,16,384]{3,2,1,0:T(8,128)}, u32[]{:S(2)}, u32[]{:S(2)}) %all-to-all-start) | async-done | bytes 1572896 | tf_op jit(solution)/shard_map/all_to_all | solution.py:59
  110.5 2.4 multiply_reduce_fusion
  113.7 0.2 fusion.8
  113.8 1.6 multiply_convert_fusion
  115.5 4.8 %convolution_convert_fusion.1 = bf16[1024,4096]{1,0:T(8,128)(2,1)S(1)} fusion(bf16[1024,384]{1,0:T(8,128)(2,1)S(1)} %bitcast.58, bf16[4096,384]{1,0:T(8,128)(2,1)S(1)} %copy-done), kind=kOutput, calls=%fused_computation.4 | convolution fusion | flops 3225419776 | bytes 12320768 | tf_op jit(solution)/shard_map/dot_general | solution.py:13
  120.3 191.4 %all_to_all.10 = bf16[32,2,16,4096]{3,2,1,0:T(8,128)(2,1)} all-to-all(bf16[32,2,16,4096]{3,2,1,0:T(8,128)(2,1)S(1)} %bitcast.55), channel_id=1, replica_groups=mesh['replica'=8,'fsdp'=32] {'fsdp'}, dimensions={0} | all-to-all | bytes 16777216 | tf_op jit(solution)/shard_map/all_to_all | solution.py:71
  311.7 12.0 %copy.18 = bf16[8,8,16,4096]{3,1,2,0:T(8,128)(2,1)} copy(bf16[8,8,16,4096]{3,2,1,0:T(8,128)(2,1)} %bitcast.53) | data formatting | bytes 16777216
  323.7 4.7 %fusion = f32[24,65536]{1,0:T(8,128)S(1)} fusion(bf16[64,65536]{1,0:T(8,128)(2,1)} %bitcast.52, s32[24]{0:T(128)S(1)} %convert_add_fusion), kind=kOutput, calls=%fused_computation.1 | convolution fusion | flops 204476928 | bytes 14680160 | tf_op jit(solution)/shard_map/dot_general | solution.py:73
  328.3 3.6 %copy.19 = f32[3,8,16,4096]{3,2,1,0:T(8,128)S(1)} copy(f32[3,8,16,4096]{3,1,2,0:T(8,128)S(1)} %bitcast.54) | data formatting | bytes 12582912
  332.0 2.6 fusion.2
  (12 shorter events, 0.0 us)
Async XLA Ops:
  7.2 1.9 copy-start
  7.2 7.4 %copy-start.4 = (s32[24]{0:T(128)S(1)}, s32[24]{0:T(128)}, u32[]{:S(2)}) copy-start(s32[24]{0:T(128)} %param.12) | copy-start | bytes 292
  7.2 45.1 %all-gather.3.cloned.1.call-start = ((), (), s32[]{:S(2)}) async-start(), calls=%async_computation.2 | async-start | bytes 5308416 | tf_op jit(solution)/shard_map/all_gather | solution.py:21
  58.9 13.3 %copy-start.2 = (s32[24,2]{0,1:T(2,128)S(1)}, s32[24,2]{0,1:T(2,128)}, u32[]{:S(2)}) copy-start(s32[24,2]{0,1:T(2,128)} %param.13) | copy-start | bytes 580
  58.9 13.3 %copy-start.3 = (f32[4,6]{1,0:T(4,128)S(1)}, f32[4,6]{1,0:T(4,128)}, u32[]{:S(2)}) copy-start(f32[4,6]{1,0:T(4,128)} %param.11) | copy-start | bytes 292
  61.0 49.6 %all-to-all-start = ((f32[32,2,16,384]{3,2,1,0:T(8,128)}), f32[32,2,16,384]{3,2,1,0:T(8,128)}, u32[]{:S(2)}, u32[]{:S(2)}) async-start(f32[32,2,16,384]{3,2,1,0:T(8,128)} %copy.14), calls=%async_computation | async-start | bytes 3145728 | tf_op jit(solution)/shard_map/all_to_all | solution.py:59
  328.3 3.7 %copy-start.1 = (bf16[24,16,4096]{2,1,0:T(8,128)(2,1)S(1)}, bf16[24,16,4096]{2,1,0:T(8,128)(2,1)}, u32[]{:S(2)}) copy-start(bf16[24,16,4096]{2,1,0:T(8,128)(2,1)} %param.7) | copy-start | bytes 9437188
Sparse Core Ops, SparseCore 0:
  14.7 37.5 all-gather.2
